TPU v7x, 256 devices: a whole 4x4x8 slice. The times are simulated.
256 devices in a mesh: req: 32 (over z_hi, x, y), cand: 8 (over z_lo, core).
Axes of the slice: x: 4, y: 4, z: 8 (z_hi: 2, z_lo: 4; z = z_hi * 4 + z_lo), core: 2. Of those that a mesh axis runs over, the one named last changes fastest.
Arguments:
- item_table: bfloat16 [32, 8, 256, 1024], P('req', 'cand'), may hold values from -25 to 25
- picked_items: int32 [32, 8, 1024], P('req', 'cand'), may hold values from 0 to 255
- destination: int32 [32, 8, 1024], P('req', 'cand'), may hold values from 0 to 31, as said below
- slot_index: int32 [32, 8, 1024], P('req', 'cand'), may hold values from 0 to 1023, as said below
- history_cache: bfloat16 [32, 8, 128, 2048], P('req', 'cand'), may hold values from -6 to 6
- history_length: int32 [32, 8], P('req'), may hold values from 16 to 128
- input_weight: bfloat16 [1024, 4096], replicated, may hold values from -0.1875 to 0.1875
- output_weight: bfloat16 [1024, 1024], replicated, may hold values from -0.1875 to 0.1875
Outputs:
- cand_out: bfloat16 [32, 8, 1024, 1024], P('req', 'cand')
Inputs may be any that keep to these rules, and one draw needn't show every extreme that they name: Each device sends exactly 1024 rows, and within each index of cand every device receives exactly 1024; no device sends more than 64 rows to one destination, and within each index of cand some device sends exactly 64 to one destination. `slot_index`: the rows that reach one device fill each of its 1024 slots exactly once.
All inputs are finite; a program needn't handle non-finite values.
Results may differ from a plain program's by a relative error of at most 0.005.
Values may be sent and summed in bfloat16 or wider, within the bound.
No kernel may reach another device: no remote copies, remote signals or barrier semaphores. Data moves between devices by JAX's collectives and lax.ppermute only.
A program may use at most 128 MiB of HBM per device.

v0:
```python
import math
import jax
import jax.numpy as jnp
from jax import lax
from jax.sharding import Mesh
from jax.sharding import PartitionSpec as P

HEADS = 8
HALVES = 2
epsilon = 1e-06


def layer_norm(values):
    average = jnp.mean(values, axis=-1, keepdims=True)
    centred = values - average
    variance = jnp.mean(centred * centred, axis=-1, keepdims=True)
    return centred * lax.rsqrt(variance + epsilon)


def attend(queries, cache_rows, lengths, head_count, score_scale):
    count_req, history_span, doubled = cache_rows.shape
    feature = doubled // 2
    head_width = feature // head_count
    keys = cache_rows[:, :, :feature].reshape(count_req, history_span, head_count, head_width)
    values = cache_rows[:, :, feature:].reshape(count_req, history_span, head_count, head_width)
    scores = (
        jnp.einsum("bihe,bjhe->bhij", queries, keys, preferred_element_type=jnp.float32)
        * score_scale
    )
    positions = jnp.arange(history_span, dtype=jnp.int32)
    valid = (positions[None, :] < lengths[:, None]).astype(jnp.float32)
    length_plus = lengths.astype(jnp.float32) + 1.0
    weights = (
        jax.nn.silu(scores) / length_plus[:, None, None, None] * valid[:, None, None, :]
    ).astype(jnp.bfloat16)
    return jnp.einsum("bhij,bjhe->bihe", weights, values, preferred_element_type=jnp.float32)


def ranks(targets, sources):
    count = targets.shape[0]
    one_hot = targets[:, None] == jnp.arange(sources, dtype=jnp.int32)[None, :]
    rows = jnp.arange(count, dtype=jnp.int32)
    lower = (rows[None, :] < rows[:, None]).astype(jnp.bfloat16)
    earlier = jnp.dot(lower, one_hot.astype(jnp.bfloat16), preferred_element_type=jnp.float32)
    return jnp.sum(jnp.where(one_hot, earlier, 0.0), axis=1).astype(jnp.int32)


def block_plan(ints, half, n_half, per_pair, sources):
    picks, targets, places = (ints[0], ints[1], ints[2])
    within = ranks(targets, sources)
    keep = targets // n_half == half
    position = jnp.where(keep, targets % n_half * per_pair + within, -1)
    spots = jnp.arange(n_half * per_pair, dtype=jnp.int32)
    hit = position[None, :] == spots[:, None]
    row = jnp.sum(jnp.where(hit, picks[None, :], 0), axis=1)
    slot = jnp.sum(jnp.where(hit, places[None, :] + 1, 0), axis=1) - 1
    return (row.reshape(n_half, per_pair), slot.reshape(n_half, per_pair))


def shards(
    item_table,
    picked_items,
    destination,
    slot_index,
    history_cache,
    history_length,
    input_weight,
    output_weight,
):
    n_half = lax.axis_size("xy")
    sources = HALVES * n_half
    half = lax.axis_index("zh")
    item_rows = item_table[0, 0]
    ints = jnp.stack([picked_items[0, 0], destination[0, 0], slot_index[0, 0]])
    slot_count = ints.shape[1]
    feature = item_rows.shape[1]
    per_pair = 2 * slot_count // sources
    swap = [(0, 1), (1, 0)]
    other_rows = lax.ppermute(item_rows, "zh", swap)
    other_ints = lax.ppermute(ints, "zh", swap)
    own_row, own_slot = block_plan(ints, half, n_half, per_pair, sources)
    far_row, far_slot = block_plan(other_ints, half, n_half, per_pair, sources)
    own_data = jnp.take(item_rows, own_row.reshape(-1), axis=0).reshape(n_half, per_pair, feature)
    far_data = jnp.take(other_rows, far_row.reshape(-1), axis=0).reshape(n_half, per_pair, feature)
    slots = jnp.concatenate([own_slot, far_slot], axis=1)
    capacity = 2 * per_pair
    radix = 32
    high = jnp.floor_divide(slots, radix)
    low = slots - high * radix
    tag_row = jnp.zeros((n_half, 8, feature), jnp.float32)
    tag_row = tag_row.at[:, 0, :capacity].set(high.astype(jnp.float32))
    tag_row = tag_row.at[:, 0, capacity : 2 * capacity].set(low.astype(jnp.float32))
    outgoing = jnp.concatenate([own_data, far_data, tag_row.astype(jnp.bfloat16)], axis=1)
    arrived = lax.all_to_all(outgoing, "xy", split_axis=0, concat_axis=0, tiled=True)
    arrived_rows = arrived[:, :capacity].reshape(n_half * capacity, feature)
    tags = (
        arrived[:, capacity, :capacity].astype(jnp.int32) * radix
        + arrived[:, capacity, capacity : 2 * capacity].astype(jnp.int32)
    ).reshape(-1)
    slot_ids = jnp.arange(slot_count, dtype=jnp.int32)
    order = jnp.arange(n_half * capacity, dtype=jnp.int32)
    fill = jnp.sum(jnp.where(tags[None, :] == slot_ids[:, None], order[None, :], 0), axis=1)
    arranged = jnp.take(arrived_rows, fill, axis=0)
    lengths = history_length[0]
    members = lengths.shape[0]
    per_request = slot_count // members
    head_count = HEADS
    head_width = feature // head_count
    score_scale = 1.0 / math.sqrt(head_width)
    as_float = arranged.astype(jnp.float32)
    normed_in = layer_norm(as_float).astype(jnp.bfloat16)
    projected = jax.nn.silu(
        jnp.dot(normed_in, input_weight, preferred_element_type=jnp.float32)
    ).astype(jnp.bfloat16)
    quarters = projected.reshape(members, per_request, 4, head_count, head_width)
    gate_u = projected[:, :feature]
    own_values = quarters[:, :, 1]
    queries = quarters[:, :, 2]
    own_keys = quarters[:, :, 3]
    length_plus = lengths.astype(jnp.float32) + 1.0
    own_scores = (
        jnp.einsum("bihe,bihe->bih", queries, own_keys, preferred_element_type=jnp.float32)
        * score_scale
    )
    own_weight = jax.nn.silu(own_scores) / length_plus[:, None, None]
    own_term = own_weight[..., None] * own_values.astype(jnp.float32)
    found = attend(
        queries,
        lax.all_gather(history_cache, "cand", axis=1, tiled=True)[0],
        lengths,
        head_count,
        score_scale,
    )
    attended = (found + own_term).reshape(slot_count, feature)
    normed_out = layer_norm(attended)
    gated = (normed_out * gate_u.astype(jnp.float32)).astype(jnp.bfloat16)
    mixed = as_float + jnp.dot(gated, output_weight, preferred_element_type=jnp.float32)
    return mixed.astype(jnp.bfloat16)[None, None]


def solution(mesh):
    n_req, n_cand = mesh.devices.shape
    devices = mesh.devices.reshape(HALVES, n_req // HALVES, n_cand)
    split = Mesh(devices, ("zh", "xy", "cand"))
    req = ("zh", "xy")
    in_specs = (
        P(req, "cand", None, None),
        P(req, "cand", None),
        P(req, "cand", None),
        P(req, "cand", None),
        P(req, "cand", None, None),
        P(req, None),
        P(),
        P(),
    )
    out_specs = P(req, "cand", None, None)
    return jax.shard_map(
        shards, mesh=split, in_specs=in_specs, out_specs=out_specs, check_vma=False
    )
```

profile of v0, /device:TPU:220, one launch (start us, length us, event | category | flops | bytes accessed | tf_op | source)
XLA Modules:
  0.0 224.5 jit_solution(4971782553543339096)
XLA Ops:
  6.5 0.9 pad_add_fusion
  7.4 0.6 collective-permute-start.1
  8.1 5.4 %collective-permute-start = (bf16[256,1024]{1,0:T(8,128)(2,1)}, bf16[256,1024]{1,0:T(8,128)(2,1)S(1)}, u32[]{:S(2)}, u32[]{:S(2)}) collective-permute-start(bf16[256,1024]{1,0:T(8,128)(2,1)} %bitcast.70), channel_id=1, source_target_pairs={{0,128},{128,0},{1,129},{129,1},{2,130},{130,2},{3,131},{131,3},{4... | collective-permute-start | bytes 1572872 | tf_op jit(solution)/shard_map/ppermute | solution.py:79
  13.5 0.7 broadcast_add_fusion
  14.1 1.3 fusion.29
  15.4 0.7 fusion.37
  16.1 1.9 select_reduce_fusion.4
  18.1 5.3 %gather_fusion.1 = bf16[1024,1024]{1,0:T(8,128)(2,1)} fusion(bf16[256,1024]{1,0:T(8,128)(2,1)S(1)} %bitcast.71, s32[1024]{0:T(1024)S(1)} %get-tuple-element.49), kind=kCustom, calls=%fused_computation.clone | custom fusion | bytes 4198400 | tf_op jit(solution)/shard_map/jit(_take)/gather | solution.py:83
  23.5 3.2 %broadcast_select_fusion.1 = bf16[1024,1024]{1,0:T(8,128)(2,1)} fusion(bf16[1024,1024]{1,0:T(8,128)(2,1)} %gather_fusion.1, pred[1024]{0:T(1024)(128)(4,1)S(1)} %compare_and_fusion.1), kind=kLoop, calls=%fused_computation.44 | loop fusion | flops 1048576 | bytes 4195328 | tf_op jit(solution)/shard_map/jit(_take)/select_n | solution.py:83
  26.7 0.7 and_reduce_fusion
  27.4 0.6 fusion.51
  28.0 0.1 concatenate.47
  28.1 0.5 fusion.28
  28.7 1.2 select_reduce_fusion.3
  29.9 0.1 concatenate.48
  30.0 0.1 fusion.48
  30.1 2.0 broadcast_select_fusion.3
  32.1 1.6 scatter.9
  33.8 3.6 %collective-permute-done = bf16[256,1024]{1,0:T(8,128)(2,1)S(1)} collective-permute-done((bf16[256,1024]{1,0:T(8,128)(2,1)}, bf16[256,1024]{1,0:T(8,128)(2,1)S(1)}, u32[]{:S(2)}, u32[]{:S(2)}) %collective-permute-start) | collective-permute-done | bytes 524320 | tf_op jit(solution)/shard_map/ppermute | solution.py:79
  37.3 5.3 %gather_fusion.2 = bf16[1024,1024]{1,0:T(8,128)(2,1)} fusion(bf16[256,1024]{1,0:T(8,128)(2,1)S(1)} %collective-permute-done, s32[1024]{0:T(1024)S(1)} %fusion.44), kind=kCustom, calls=%fused_computation.1.clone | custom fusion | bytes 4198400 | tf_op jit(solution)/shard_map/jit(_take)/gather | solution.py:84
  42.7 2.0 broadcast_select_fusion
  44.7 0.2 copy-done.4
  44.9 2.3 %pad_maximum_fusion = bf16[16,136,1024]{2,1,0:T(8,128)(2,1)} fusion(bf16[16,8,1024]{2,1,0:T(8,128)(2,1)S(1)} %scatter.9, bf16[16,64,1024]{2,1,0:T(8,128)(2,1)S(1)} %bitcast.77, bf16[16,64,1024]{2,1,0:T(8,128)(2,1)S(1)} %bitcast.76), kind=kLoop, calls=%fused_computation.11 | loop fusion | flops 13369344 | bytes 8912896 | tf_op jit(solution)/shard_map/concatenate | solution.py:93
  47.2 7.2 %all-to-all-start = ((bf16[16,136,1024]{2,1,0:T(8,128)(2,1)}), bf16[16,136,1024]{2,1,0:T(8,128)(2,1)}, u32[]{:S(2)}, u32[]{:S(2)}) async-start(bf16[16,136,1024]{2,1,0:T(8,128)(2,1)} %pad_maximum_fusion), calls=%async_computation | async-start | bytes 8912896 | tf_op jit(solution)/shard_map/all_to_all | solution.py:94
  54.5 0.0 all-gather.2.cloned.1.call-start
  54.5 0.7 all-gather.2.cloned.1.call-update
  55.2 0.1 fusion.41
  55.3 67.1 %all-to-all-done = bf16[16,136,1024]{2,1,0:T(8,128)(2,1)} async-done(((bf16[16,136,1024]{2,1,0:T(8,128)(2,1)}), bf16[16,136,1024]{2,1,0:T(8,128)(2,1)}, u32[]{:S(2)}, u32[]{:S(2)}) %all-to-all-start) | async-done | bytes 4456480 | tf_op jit(solution)/shard_map/all_to_all | solution.py:94
  122.3 4.8 %slice.113 = bf16[16,128,1024]{2,1,0:T(8,128)(2,1)} slice(bf16[16,136,1024]{2,1,0:T(8,128)(2,1)} %all-to-all-done), slice={[0:16], [0:128], [0:1024]} | slice | bytes 8388608 | tf_op jit(solution)/shard_map/slice | solution.py:95
  127.1 0.8 fusion.32
  127.9 0.9 select_reduce_fusion
  128.8 8.9 %gather_fusion = bf16[1024,1024]{1,0:T(8,128)(2,1)} fusion(bf16[2048,1024]{1,0:T(8,128)(2,1)} %bitcast.72, s32[1024]{0:T(1024)S(1)} %broadcast_clamp_fusion), kind=kCustom, calls=%fused_computation.2 | custom fusion | bytes 4198400 | tf_op jit(solution)/shard_map/jit(_take)/gather | solution.py:103
  137.8 2.3 %convert_reduce_fusion = f32[1024]{0:T(1024)S(1)} fusion(bf16[1024,1024]{1,0:T(8,128)(2,1)} %gather_fusion, pred[1024]{0:T(1024)(128)(4,1)S(1)} %compare_and_fusion.2), kind=kLoop, calls=%fused_computation.8 | loop fusion | flops 3144704 | bytes 2102272 | tf_op jit(solution)/shard_map/reduce_sum | solution.py:14
  140.1 2.4 %fusion.2 = f32[1024]{0:T(1024)S(1)} fusion(f32[1024]{0:T(1024)S(1)} %broadcast_multiply_fusion.1, bf16[1024,1024]{1,0:T(8,128)(2,1)} %gather_fusion, pred[1024]{0:T(1024)(128)(4,1)S(1)} %compare_and_fusion.2), kind=kLoop, calls=%fused_computation.12 | loop fusion | flops 5241856 | bytes 2106368 | tf_op jit(solution)/shard_map/reduce_sum | solution.py:16
  142.6 15.8 %multiply_convert_fusion = bf16[1024,4096]{1,0:T(8,128)(2,1)} fusion(bf16[1024,4096]{1,0:T(8,128)(2,1)} %param.20, f32[1024]{0:T(1024)S(1)} %add_rsqrt_fusion, f32[1024]{0:T(1024)S(1)} %broadcast_multiply_fusion.1, bf16[1024,1024]{1,0:T(8,128)(2,1)S(1)} %copy-done.2, pred[1024]{0:T(1024)(128)(4,1)S(1)} %compare_and_fusion.2), kind=kOutput, calls=%fused_computation.3 | convolution fusion | flops 8616148992 | bytes 18883584 | tf_op jit(solution)/shard_map/dot_general | solution.py:113
  158.4 9.4 %copy.38 = bf16[128,8,32,128]{3,2,1,0:T(8,128)(2,1)} copy(bf16[128,8,32,128]{3,1,2,0:T(8,128)(2,1)} %bitcast.78) | data formatting | bytes 16777216
  167.8 4.8 %fusion.49 = (bf16[8,128,1,8,128]{4,3,2,1,0:T(8,128)(2,1)}, bf16[8,128,1,8,128]{4,3,2,1,0:T(8,128)(2,1)}) fusion(bf16[8,128,4,8,128]{4,3,2,1,0:T(8,128)(2,1)} %bitcast.73), kind=kLoop, calls=%fused_computation.115 | loop fusion | bytes 8388608 | tf_op jit(solution)/shard_map/slice | solution.py:118
  172.6 4.1 %copy.37 = bf16[8,128,1,8,128]{1,4,3,0,2:T(8,128)(2,1)} copy(bf16[8,128,1,8,128]{4,3,2,1,0:T(8,128)(2,1)} %get-tuple-element.37) | data formatting | bytes 4194304
  176.7 2.1 fusion.23
  178.9 4.2 %multiply_reduce_fusion = f32[8,128,8]{2,1,0:T(8,128)S(1)} fusion(f32[8,128,8,128]{3,1,2,0:T(8,128)S(1)} %fusion.23, bf16[8,128,4,8,128]{4,3,2,1,0:T(8,128)(2,1)} %bitcast.74), kind=kLoop, calls=%fused_computation.21 | loop fusion | flops 3137536 | bytes 6324224
  183.0 0.2 copy.35
  183.2 0.1 multiply_divide_fusion
  183.3 6.5 %copy.26 = bf16[1,8,128,2048]{2,3,1,0:T(8,128)(2,1)} copy(bf16[1,8,128,2048]{3,2,0,1:T(8,128)(2,1)} %all-gather.2.cloned.1.call-done) | data formatting | bytes 8388608 | tf_op jit(solution)/shard_map/all_gather | solution.py:129
  189.8 4.6 %fusion.50 = (bf16[8,128,1024]{1,2,0:T(8,128)(2,1)}, bf16[8,128,1024]{1,2,0:T(8,128)(2,1)}) fusion(bf16[8,128,2048]{1,2,0:T(8,128)(2,1)} %bitcast.75), kind=kLoop, calls=%fused_computation.116 | loop fusion | bytes 8388608 | tf_op jit(solution)/shard_map/slice | solution.py:24
  194.4 8.2 %fusion.52 = (f32[8,128]{1,0:T(8,128)S(1)}, f32[8,128,8,128]{1,3,2,0:T(8,128)}) fusion(bf16[8,128,1,8,128]{1,4,3,0,2:T(8,128)(2,1)} %copy.37, f32[8,128,8]{1,2,0:T(8,128)S(1)} %multiply_divide_fusion, bf16[8,128,8,128]{1,3,2,0:T(8,128)(2,1)} %bitcast.81, bf16[8,128,8,128]{1,3,2,0:T(8,128)(2,1)} %bitcast.80, f32[8,128]{1,0:T(8,128)S(1)} %fusion.41, ...), kind=kOutput, calls=%fused_computation.118 | convolution fusion | flops 549452800 | bytes 12623904 | tf_op jit(solution)/shard_map/bhij,bjhe->bihe/dot_general | solution.py:36
  202.6 5.4 %copy.29 = f32[8,128,8,128]{3,2,1,0:T(8,128)} copy(f32[8,128,8,128]{1,3,2,0:T(8,128)} %get-tuple-element.48) | data formatting | bytes 8388608 | tf_op jit(solution)/shard_map/add | solution.py:134
  208.0 2.8 %multiply_reduce_fusion.1 = f32[8,128]{1,0:T(8,128)S(1)} fusion(f32[8,128,8,128]{1,3,2,0:T(8,128)} %get-tuple-element.48, f32[8,128]{1,0:T(8,128)S(1)} %get-tuple-element.44), kind=kLoop, calls=%fused_computation.22 | loop fusion | flops 3144704 | bytes 4202496 | tf_op jit(solution)/shard_map/reduce_sum | solution.py:16
  210.8 6.8 %fusion.13 = bf16[1,1,1024,1024]{3,2,1,0:T(8,128)(2,1)} fusion(bf16[1024,1024]{1,0:T(8,128)(2,1)S(1)} %copy-done, f32[128,8,8,128]{3,2,1,0:T(8,128)} %bitcast.79, bf16[1024,4096]{1,0:T(8,128)(2,1)} %multiply_convert_fusion, f32[1024]{0:T(1024)S(1)} %rsqrt_bitcast_fusion, f32[1024]{0:T(1024)S(1)} %get-tuple-element.43, bf16[1024,1024]{1,0:T(8,128)(2,1)S(1)} %copy-done.3, ...), kind=kOutput, calls=%fused_computation.34 | convolution fusion | flops 2156920832 | bytes 12592128 | tf_op jit(solution)/shard_map/dot_general | solution.py:137
  (33 shorter events, 0.2 us)
Async XLA Ops:
  6.5 204.3 %copy-start = (bf16[1024,1024]{1,0:T(8,128)(2,1)S(1)}, bf16[1024,1024]{1,0:T(8,128)(2,1)}, u32[]{:S(2)}) copy-start(bf16[1024,1024]{1,0:T(8,128)(2,1)} %param.21) | copy-start | bytes 6291460
  6.5 11.6 %copy-start.1 = (bf16[1,1,256,1024]{3,2,1,0:T(8,128)(2,1)S(1)}, bf16[1,1,256,1024]{3,2,1,0:T(8,128)(2,1)}, u32[]{:S(2)}) copy-start(bf16[1,1,256,1024]{3,2,1,0:T(8,128)(2,1)} %param.14) | copy-start | bytes 1572868
  7.4 20.6 %collective-permute-start.1 = (s32[3,1024]{1,0:T(4,128)S(1)}, s32[3,1024]{1,0:T(4,128)S(1)}, u32[]{:S(2)}, u32[]{:S(2)}) collective-permute-start(s32[3,1024]{1,0:T(4,128)S(1)} %pad_add_fusion), channel_id=1, source_target_pairs={{0,128},{128,0},{1,129},{129,1},{2,130},{130,2},{3,131},{131,3},{4... | collective-permute-start | bytes 36872 | tf_op jit(solution)/shard_map/ppermute | solution.py:80
  8.1 29.3 %collective-permute-start = (bf16[256,1024]{1,0:T(8,128)(2,1)}, bf16[256,1024]{1,0:T(8,128)(2,1)S(1)}, u32[]{:S(2)}, u32[]{:S(2)}) collective-permute-start(bf16[256,1024]{1,0:T(8,128)(2,1)} %bitcast.70), channel_id=1, source_target_pairs={{0,128},{128,0},{1,129},{129,1},{2,130},{130,2},{3,131},{131,3},{4... | collective-permute-start | bytes 1572872 | tf_op jit(solution)/shard_map/ppermute | solution.py:79
  23.5 3.2 %copy-start.6 = (s32[3]{0:T(128)S(1)}, s32[3]{0:T(128)}, u32[]{:S(2)}) copy-start(s32[3]{0:T(128)} %constant.161.clone.1) | copy-start | bytes 40
  42.7 2.2 copy-start.4
  47.2 8.0 %copy-start.5 = (s32[1,8]{1,0:T(1,128)S(1)}, s32[1,8]{1,0:T(1,128)}, u32[]{:S(2)}) copy-start(s32[1,8]{1,0:T(1,128)} %param.19) | copy-start | bytes 100
  47.2 75.1 %all-to-all-start = ((bf16[16,136,1024]{2,1,0:T(8,128)(2,1)}), bf16[16,136,1024]{2,1,0:T(8,128)(2,1)}, u32[]{:S(2)}, u32[]{:S(2)}) async-start(bf16[16,136,1024]{2,1,0:T(8,128)(2,1)} %pad_maximum_fusion), calls=%async_computation | async-start | bytes 8912896 | tf_op jit(solution)/shard_map/all_to_all | solution.py:94
  54.5 128.9 %all-gather.2.cloned.1.call-start = ((), (), s32[]{:S(2)}) async-start(), calls=%async_computation.1 | async-start | bytes 4718592 | tf_op jit(solution)/shard_map/all_gather | solution.py:129
  137.8 4.8 %copy-start.2 = (bf16[1024,1024]{1,0:T(8,128)(2,1)S(1)}, bf16[1024,1024]{1,0:T(8,128)(2,1)}, u32[]{:S(2)}) copy-start(bf16[1024,1024]{1,0:T(8,128)(2,1)} %gather_fusion) | copy-start | bytes 6291460
  208.0 2.9 %copy-start.3 = (bf16[1024,1024]{1,0:T(8,128)(2,1)S(1)}, bf16[1024,1024]{1,0:T(8,128)(2,1)}, u32[]{:S(2)}) copy-start(bf16[1024,1024]{1,0:T(8,128)(2,1)} %gather_fusion) | copy-start | bytes 6291460
Sparse Core Ops, SparseCore 0:
  57.0 52.5 all-gather.1
where the time goes:
time: 225 us; the launch traced here: 224 us
  waiting for transfers between devices  71.3 us (32%)
  local copies, waits for them, and re-layouts  61.9 us (28%)
  matrix products  32.6 us (14%)
  other arithmetic  31.7 us (14%)
  between operations  13.6 us (6%)
  starting transfers between devices  13.3 us (6%)
    all_to_all x1, waiting for transfers between devices, shards(): lax.all_to_all(outgoing, 'xy', split_axis=0, concat_axis=0, tiled=True)  67.1 us
    dot_general x1, matrix products, shards(): jnp.dot(normed_in, input_weight, preferred_element_type=jnp.float32)  15.8 us
    unnamed x16, local copies, waits for them, and re-layouts  13.8 us
    gather x1, local copies, waits for them, and re-layouts, shards(): arranged = jnp.take(arrived_rows, fill, axis=0)  8.92 us
    dot_general x1, matrix products, attend(): jnp.einsum('bhij,bjhe->bihe', weights, values, preferred_element_type=jnp...  8.22 us
    all_to_all x1, starting transfers between devices, shards(): lax.all_to_all(outgoing, 'xy', split_axis=0, concat_axis=0, tiled=True)  7.24 us
    dot_general x1, matrix products, shards(): jnp.dot(gated, output_weight, preferred_element_type=jnp.float32)  6.8 us
    all_gather x1, local copies, waits for them, and re-layouts, shards(): lax.all_gather(history_cache, 'cand', axis=1, tiled=True)[0]  6.47 us
  transfers between devices with their start and end apart: 4, of which 2 were waited for; matrix products, arithmetic and copies ran while one was open for 36% of the time, Pallas kernels for 0%

commit v1 on v0

--- a/solution.py
+++ b/solution.py
@@ -126,7 +126,9 @@
     own_term = own_weight[..., None] * own_values.astype(jnp.float32)
     found = attend(
         queries,
-        lax.all_gather(history_cache, "cand", axis=1, tiled=True)[0],
+        jnp.concatenate(
+            lax.all_to_all(jnp.stack([history_cache] * lax.axis_size("cand")), "cand", 0, 0), axis=1
+        )[0],
         lengths,
         head_count,
         score_scale,

time: 225 us -> 245 us (1.089); the launches traced: 224 us -> 241 us
  waiting for transfers between devices: 71.3 us -> 101 us
  between operations: 13.6 us -> 0.25 us
  starting transfers between devices: 13.3 us -> 17.9 us
  local copies, waits for them, and re-layouts: 61.9 us -> 57.9 us
    all_to_all x0 -> x1, waiting for transfers between devices: none -> 29.6 us  [shards(): lax.all_to_all(jnp.stack([history_cache] * lax.axis_size('cand')), 'cand'...]
    all_gather x1 -> x0, local copies, waits for them, and re-layouts: 6.47 us -> none  [shards(): lax.all_gather(history_cache, 'cand', axis=1, tiled=True)[0]]
    all_to_all x0 -> x1, starting transfers between devices: none -> 4.67 us  [shards(): lax.all_to_all(jnp.stack([history_cache] * lax.axis_size('cand')), 'cand'...]
    another operation x1 -> x3, local copies, waits for them, and re-layouts: 0.59 us -> 3.37 us  [the longest x1 2.51 us: shards(): jnp.stack([history_cache] * lax.axis_size('cand'))]
    unnamed x16 -> x18, local copies, waits for them, and re-layouts: 13.8 us -> 13.8 us
  transfers between devices with their start and end apart: 4 -> 4, of which waited for: 2 -> 3; matrix products, arithmetic and copies ran while one was open for 36% -> 34% of each run, Pallas kernels for 0% -> 0%
where the time goes in v1:
time: 245 us; the launch traced here: 241 us
  waiting for transfers between devices  101 us (41%)
  local copies, waits for them, and re-layouts  57.9 us (24%)
  matrix products  32.7 us (13%)
  other arithmetic  31.7 us (13%)
  starting transfers between devices  17.9 us (7%)
    all_to_all x1, waiting for transfers between devices, shards(): lax.all_to_all(outgoing, 'xy', split_axis=0, concat_axis=0, tiled=True)  67.5 us
    all_to_all x1, waiting for transfers between devices, shards(): lax.all_to_all(jnp.stack([history_cache] * lax.axis_size('cand')), 'cand'...  29.6 us
    dot_general x1, matrix products, shards(): jnp.dot(normed_in, input_weight, preferred_element_type=jnp.float32)  15.8 us
    unnamed x18, local copies, waits for them, and re-layouts  13.8 us
    gather x1, local copies, waits for them, and re-layouts, shards(): arranged = jnp.take(arrived_rows, fill, axis=0)  8.74 us
    dot_general x1, matrix products, attend(): jnp.einsum('bhij,bjhe->bihe', weights, values, preferred_element_type=jnp...  8.23 us
    all_to_all x1, starting transfers between devices, shards(): lax.all_to_all(outgoing, 'xy', split_axis=0, concat_axis=0, tiled=True)  7.24 us
    dot_general x1, matrix products, shards(): jnp.dot(gated, output_weight, preferred_element_type=jnp.float32)  6.81 us
  transfers between devices with their start and end apart: 4, of which 3 were waited for; matrix products, arithmetic and copies ran while one was open for 34% of the time, Pallas kernels for 0%

profile of v1, /device:TPU:220, one launch (start us, length us, event | category | flops | bytes accessed | tf_op | source)
XLA Modules:
  0.0 241.1 jit_solution(1913103585225898523)
XLA Ops:
  0.0 0.9 pad_add_fusion
  0.9 0.6 collective-permute-start.1
  1.5 5.4 %collective-permute-start = (bf16[256,1024]{1,0:T(8,128)(2,1)}, bf16[256,1024]{1,0:T(8,128)(2,1)S(1)}, u32[]{:S(2)}, u32[]{:S(2)}) collective-permute-start(bf16[256,1024]{1,0:T(8,128)(2,1)} %bitcast.70), channel_id=1, source_target_pairs={{0,128},{128,0},{1,129},{129,1},{2,130},{130,2},{3,131},{131,3},{4... | collective-permute-start | bytes 1572872 | tf_op jit(solution)/shard_map/ppermute | solution.py:79
  6.9 0.7 broadcast_add_fusion
  7.6 1.3 fusion.29
  8.9 0.7 fusion.37
  9.6 1.9 select_reduce_fusion.4
  11.6 5.3 %gather_fusion.1 = bf16[1024,1024]{1,0:T(8,128)(2,1)} fusion(bf16[256,1024]{1,0:T(8,128)(2,1)S(1)} %bitcast.71, s32[1024]{0:T(1024)S(1)} %get-tuple-element.49), kind=kCustom, calls=%fused_computation.clone | custom fusion | bytes 4198400 | tf_op jit(solution)/shard_map/jit(_take)/gather | solution.py:83
  16.9 3.2 %broadcast_select_fusion.1 = bf16[1024,1024]{1,0:T(8,128)(2,1)} fusion(bf16[1024,1024]{1,0:T(8,128)(2,1)} %gather_fusion.1, pred[1024]{0:T(1024)(128)(4,1)S(1)} %compare_and_fusion.1), kind=kLoop, calls=%fused_computation.44 | loop fusion | flops 1048576 | bytes 4195328 | tf_op jit(solution)/shard_map/jit(_take)/select_n | solution.py:83
  20.1 0.7 and_reduce_fusion
  20.9 0.6 fusion.51
  21.4 0.1 concatenate.47
  21.5 0.5 fusion.28
  22.1 1.2 select_reduce_fusion.3
  23.4 0.1 concatenate.48
  23.5 0.1 fusion.48
  23.6 2.0 broadcast_select_fusion.3
  25.6 1.6 scatter.9
  27.2 3.6 %collective-permute-done = bf16[256,1024]{1,0:T(8,128)(2,1)S(1)} collective-permute-done((bf16[256,1024]{1,0:T(8,128)(2,1)}, bf16[256,1024]{1,0:T(8,128)(2,1)S(1)}, u32[]{:S(2)}, u32[]{:S(2)}) %collective-permute-start) | collective-permute-done | bytes 524320 | tf_op jit(solution)/shard_map/ppermute | solution.py:79
  30.8 5.3 %gather_fusion.2 = bf16[1024,1024]{1,0:T(8,128)(2,1)} fusion(bf16[256,1024]{1,0:T(8,128)(2,1)S(1)} %collective-permute-done, s32[1024]{0:T(1024)S(1)} %fusion.44), kind=kCustom, calls=%fused_computation.1.clone | custom fusion | bytes 4198400 | tf_op jit(solution)/shard_map/jit(_take)/gather | solution.py:84
  36.1 2.0 broadcast_select_fusion
  38.1 0.2 copy-done.4
  38.4 2.3 pad_maximum_fusion
  40.7 7.2 %all-to-all-start = ((bf16[16,136,1024]{2,1,0:T(8,128)(2,1)}), bf16[16,136,1024]{2,1,0:T(8,128)(2,1)}, u32[]{:S(2)}, u32[]{:S(2)}) async-start(bf16[16,136,1024]{2,1,0:T(8,128)(2,1)} %pad_maximum_fusion), calls=%async_computation | async-start | bytes 8912896 | tf_op jit(solution)/shard_map/all_to_all | solution.py:94
  47.9 0.3 copy.24
  48.3 67.5 %all-to-all-done = bf16[16,136,1024]{2,1,0:T(8,128)(2,1)} async-done(((bf16[16,136,1024]{2,1,0:T(8,128)(2,1)}), bf16[16,136,1024]{2,1,0:T(8,128)(2,1)}, u32[]{:S(2)}, u32[]{:S(2)}) %all-to-all-start) | async-done | bytes 4456480 | tf_op jit(solution)/shard_map/all_to_all | solution.py:94
  115.8 2.5 %stack.5 = bf16[8,1,1,128,2048]{3,4,2,1,0:T(8,128)(2,1)} broadcast(bf16[128,2048]{0,1:T(8,128)(2,1)S(1)} %copy.24), dimensions={3,4} | broadcast | bytes 4718592 | tf_op jit(solution)/shard_map/stack | solution.py:130
  118.3 4.7 %all-to-all-start.1 = ((bf16[8,1,1,128,2048]{3,4,2,1,0:T(8,128)(2,1)}), bf16[8,1,1,128,2048]{3,4,2,1,0:T(8,128)(2,1)}, u32[]{:S(2)}, u32[]{:S(2)}) async-start(bf16[8,1,1,128,2048]{3,4,2,1,0:T(8,128)(2,1)} %stack.5), calls=%async_computation.1 | async-start | bytes 8388608 | tf_op jit(solution)/shard_map/all_to_all | solution.py:130
  123.0 4.8 %slice.113 = bf16[16,128,1024]{2,1,0:T(8,128)(2,1)} slice(bf16[16,136,1024]{2,1,0:T(8,128)(2,1)} %all-to-all-done), slice={[0:16], [0:128], [0:1024]} | slice | bytes 8388608 | tf_op jit(solution)/shard_map/slice | solution.py:95
  127.8 0.8 fusion.32
  128.6 0.9 select_reduce_fusion
  129.5 8.7 %gather_fusion = bf16[1024,1024]{1,0:T(8,128)(2,1)} fusion(bf16[2048,1024]{1,0:T(8,128)(2,1)} %bitcast.72, s32[1024]{0:T(1024)S(1)} %broadcast_clamp_fusion), kind=kCustom, calls=%fused_computation.2 | custom fusion | bytes 4198400 | tf_op jit(solution)/shard_map/jit(_take)/gather | solution.py:103
  138.3 2.3 convert_reduce_fusion
  140.6 2.4 %fusion.2 = f32[1024]{0:T(1024)S(1)} fusion(f32[1024]{0:T(1024)S(1)} %broadcast_multiply_fusion.1, bf16[1024,1024]{1,0:T(8,128)(2,1)} %gather_fusion, pred[1024]{0:T(1024)(128)(4,1)S(1)} %compare_and_fusion.2), kind=kLoop, calls=%fused_computation.12 | loop fusion | flops 5241856 | bytes 2106368 | tf_op jit(solution)/shard_map/reduce_sum | solution.py:16
  143.1 15.8 %multiply_convert_fusion = bf16[1024,4096]{1,0:T(8,128)(2,1)} fusion(bf16[1024,4096]{1,0:T(8,128)(2,1)} %param.20, f32[1024]{0:T(1024)S(1)} %add_rsqrt_fusion, f32[1024]{0:T(1024)S(1)} %broadcast_multiply_fusion.1, bf16[1024,1024]{1,0:T(8,128)(2,1)S(1)} %copy-done.2, pred[1024]{0:T(1024)(128)(4,1)S(1)} %compare_and_fusion.2), kind=kOutput, calls=%fused_computation.3 | convolution fusion | flops 8616148992 | bytes 18883584 | tf_op jit(solution)/shard_map/dot_general | solution.py:113
  158.9 9.4 %copy.36 = bf16[128,8,32,128]{3,2,1,0:T(8,128)(2,1)} copy(bf16[128,8,32,128]{3,1,2,0:T(8,128)(2,1)} %bitcast.77) | data formatting | bytes 16777216
  168.3 4.6 %fusion.49 = (bf16[8,128,1,8,128]{4,3,2,1,0:T(8,128)(2,1)}, bf16[8,128,1,8,128]{4,3,2,1,0:T(8,128)(2,1)}) fusion(bf16[8,128,4,8,128]{4,3,2,1,0:T(8,128)(2,1)} %bitcast.73), kind=kLoop, calls=%fused_computation.115 | loop fusion | bytes 8388608 | tf_op jit(solution)/shard_map/slice | solution.py:118
  172.9 4.1 %copy.35 = bf16[8,128,1,8,128]{1,4,3,0,2:T(8,128)(2,1)} copy(bf16[8,128,1,8,128]{4,3,2,1,0:T(8,128)(2,1)} %get-tuple-element.37) | data formatting | bytes 4194304
  177.1 2.1 fusion.23
  179.2 4.2 %multiply_reduce_fusion = f32[8,128,8]{2,1,0:T(8,128)S(1)} fusion(f32[8,128,8,128]{3,1,2,0:T(8,128)S(1)} %fusion.23, bf16[8,128,4,8,128]{4,3,2,1,0:T(8,128)(2,1)} %bitcast.74), kind=kLoop, calls=%fused_computation.21 | loop fusion | flops 3137536 | bytes 6324224
  183.4 0.2 copy.33
  183.5 0.1 multiply_divide_fusion
  183.6 29.6 %all-to-all-done.1 = bf16[8,1,1,128,2048]{3,4,2,1,0:T(8,128)(2,1)} async-done(((bf16[8,1,1,128,2048]{3,4,2,1,0:T(8,128)(2,1)}), bf16[8,1,1,128,2048]{3,4,2,1,0:T(8,128)(2,1)}, u32[]{:S(2)}, u32[]{:S(2)}) %all-to-all-start.1) | async-done | bytes 4194336 | tf_op jit(solution)/shard_map/all_to_all | solution.py:130
  213.2 4.6 %fusion.50 = (bf16[8,128,1024]{1,2,0:T(8,128)(2,1)}, bf16[8,128,1024]{1,2,0:T(8,128)(2,1)}) fusion(bf16[8,128,2048]{1,2,0:T(8,128)(2,1)} %bitcast.22), kind=kLoop, calls=%fused_computation.116 | loop fusion | bytes 8388608 | tf_op jit(solution)/shard_map/slice | solution.py:24
  217.8 8.2 %fusion.52 = (f32[8,128]{1,0:T(8,128)S(1)}, f32[8,128,8,128]{1,3,2,0:T(8,128)}) fusion(bf16[8,128,1,8,128]{1,4,3,0,2:T(8,128)(2,1)} %copy.35, f32[8,128,8]{1,2,0:T(8,128)S(1)} %multiply_divide_fusion, bf16[8,128,8,128]{1,3,2,0:T(8,128)(2,1)} %bitcast.80, bf16[8,128,8,128]{1,3,2,0:T(8,128)(2,1)} %bitcast.79, f32[8,128]{1,0:T(8,128)S(1)} %fusion.41, ...), kind=kOutput, calls=%fused_computation.118 | convolution fusion | flops 549452800 | bytes 12623904 | tf_op jit(solution)/shard_map/bhij,bjhe->bihe/dot_general | solution.py:36
  226.0 5.4 %copy.27 = f32[8,128,8,128]{3,2,1,0:T(8,128)} copy(f32[8,128,8,128]{1,3,2,0:T(8,128)} %get-tuple-element.48) | data formatting | bytes 8388608 | tf_op jit(solution)/shard_map/add | solution.py:136
  231.4 2.8 %multiply_reduce_fusion.1 = f32[8,128]{1,0:T(8,128)S(1)} fusion(f32[8,128,8,128]{1,3,2,0:T(8,128)} %get-tuple-element.48, f32[8,128]{1,0:T(8,128)S(1)} %get-tuple-element.44), kind=kLoop, calls=%fused_computation.22 | loop fusion | flops 3144704 | bytes 4202496 | tf_op jit(solution)/shard_map/reduce_sum | solution.py:16
  234.3 6.8 %fusion.13 = bf16[1,1,1024,1024]{3,2,1,0:T(8,128)(2,1)} fusion(bf16[1024,1024]{1,0:T(8,128)(2,1)S(1)} %copy-done, f32[128,8,8,128]{3,2,1,0:T(8,128)} %bitcast.78, bf16[1024,4096]{1,0:T(8,128)(2,1)} %multiply_convert_fusion, f32[1024]{0:T(1024)S(1)} %rsqrt_bitcast_fusion, f32[1024]{0:T(1024)S(1)} %get-tuple-element.43, bf16[1024,1024]{1,0:T(8,128)(2,1)S(1)} %copy-done.3, ...), kind=kOutput, calls=%fused_computation.34 | convolution fusion | flops 2156920832 | bytes 12592128 | tf_op jit(solution)/shard_map/dot_general | solution.py:139
  (35 shorter events, 0.3 us)
Async XLA Ops:
  0.0 234.2 %copy-start = (bf16[1024,1024]{1,0:T(8,128)(2,1)S(1)}, bf16[1024,1024]{1,0:T(8,128)(2,1)}, u32[]{:S(2)}) copy-start(bf16[1024,1024]{1,0:T(8,128)(2,1)} %param.21) | copy-start | bytes 6291460
  0.0 11.6 %copy-start.1 = (bf16[1,1,256,1024]{3,2,1,0:T(8,128)(2,1)S(1)}, bf16[1,1,256,1024]{3,2,1,0:T(8,128)(2,1)}, u32[]{:S(2)}) copy-start(bf16[1,1,256,1024]{3,2,1,0:T(8,128)(2,1)} %param.14) | copy-start | bytes 1572868
  0.9 20.6 %collective-permute-start.1 = (s32[3,1024]{1,0:T(4,128)S(1)}, s32[3,1024]{1,0:T(4,128)S(1)}, u32[]{:S(2)}, u32[]{:S(2)}) collective-permute-start(s32[3,1024]{1,0:T(4,128)S(1)} %pad_add_fusion), channel_id=1, source_target_pairs={{0,128},{128,0},{1,129},{129,1},{2,130},{130,2},{3,131},{131,3},{4... | collective-permute-start | bytes 36872 | tf_op jit(solution)/shard_map/ppermute | solution.py:80
  1.5 29.3 %collective-permute-start = (bf16[256,1024]{1,0:T(8,128)(2,1)}, bf16[256,1024]{1,0:T(8,128)(2,1)S(1)}, u32[]{:S(2)}, u32[]{:S(2)}) collective-permute-start(bf16[256,1024]{1,0:T(8,128)(2,1)} %bitcast.70), channel_id=1, source_target_pairs={{0,128},{128,0},{1,129},{129,1},{2,130},{130,2},{3,131},{131,3},{4... | collective-permute-start | bytes 1572872 | tf_op jit(solution)/shard_map/ppermute | solution.py:79
  16.9 3.2 %copy-start.7 = (s32[3]{0:T(128)S(1)}, s32[3]{0:T(128)}, u32[]{:S(2)}) copy-start(s32[3]{0:T(128)} %constant.161.clone.1) | copy-start | bytes 40
  36.1 2.2 copy-start.4
  40.7 7.3 %copy-start.5 = (bf16[1,1,128,2048]{3,2,1,0:T(8,128)(2,1)S(1)}, bf16[1,1,128,2048]{3,2,1,0:T(8,128)(2,1)}, u32[]{:S(2)}) copy-start(bf16[1,1,128,2048]{3,2,1,0:T(8,128)(2,1)} %param.18) | copy-start | bytes 1572868
  40.7 7.5 %copy-start.6 = (s32[1,8]{1,0:T(1,128)S(1)}, s32[1,8]{1,0:T(1,128)}, u32[]{:S(2)}) copy-start(s32[1,8]{1,0:T(1,128)} %param.19) | copy-start | bytes 100
  40.7 75.1 %all-to-all-start = ((bf16[16,136,1024]{2,1,0:T(8,128)(2,1)}), bf16[16,136,1024]{2,1,0:T(8,128)(2,1)}, u32[]{:S(2)}, u32[]{:S(2)}) async-start(bf16[16,136,1024]{2,1,0:T(8,128)(2,1)} %pad_maximum_fusion), calls=%async_computation | async-start | bytes 8912896 | tf_op jit(solution)/shard_map/all_to_all | solution.py:94
  118.3 94.9 %all-to-all-start.1 = ((bf16[8,1,1,128,2048]{3,4,2,1,0:T(8,128)(2,1)}), bf16[8,1,1,128,2048]{3,4,2,1,0:T(8,128)(2,1)}, u32[]{:S(2)}, u32[]{:S(2)}) async-start(bf16[8,1,1,128,2048]{3,4,2,1,0:T(8,128)(2,1)} %stack.5), calls=%async_computation.1 | async-start | bytes 8388608 | tf_op jit(solution)/shard_map/all_to_all | solution.py:130
  138.3 4.8 %copy-start.2 = (bf16[1024,1024]{1,0:T(8,128)(2,1)S(1)}, bf16[1024,1024]{1,0:T(8,128)(2,1)}, u32[]{:S(2)}) copy-start(bf16[1024,1024]{1,0:T(8,128)(2,1)} %gather_fusion) | copy-start | bytes 6291460
  231.4 2.9 %copy-start.3 = (bf16[1024,1024]{1,0:T(8,128)(2,1)S(1)}, bf16[1024,1024]{1,0:T(8,128)(2,1)}, u32[]{:S(2)}) copy-start(bf16[1024,1024]{1,0:T(8,128)(2,1)} %gather_fusion) | copy-start | bytes 6291460
